TPU v7x, 256 devices: a whole 4x4x8 slice. The times are simulated.
256 devices in a mesh: rows: 64 (over z, y, x_hi), cent: 4 (over x_lo, core).
Axes of the slice: x: 4 (x_hi: 2, x_lo: 2; x = x_hi * 2 + x_lo), y: 4, z: 8, core: 2. Of those that a mesh axis runs over, the one named last changes fastest.
Arguments:
- embeddings: bfloat16 [131072, 4096], P('rows', 'cent'), may hold values from -6 to 6
- basis: bfloat16 [4096, 512], P('cent'), may hold values from -0.09375 to 0.09375
- start_centroids: float32 [4096, 512], P('cent'), as said below
Outputs:
- centroids: float32 [4096, 512], P('cent')
- log_total: float32 [131072], P('rows')
Inputs may be any that keep to these rules, and one draw needn't show every extreme that they name: `start_centroids`: initial centroids, real-valued; some may lie far from the others.
All inputs are finite; a program needn't handle non-finite values.
Results may differ from a plain program's by a relative error of at most 0.0024.
The roundings to bfloat16 on the way count: a program that leaves them out, or rounds other values in their place, can miss the bound.
Values may be sent and summed in bfloat16 or wider, within the bound.
No kernel may reach another device: no remote copies, remote signals or barrier semaphores. Data moves between devices by JAX's collectives and lax.ppermute only.
A program may use at most 64 MiB of HBM per device.

v0:
```python
import jax
import jax.numpy as jnp
from jax import lax
from jax.sharding import Mesh
from jax.sharding import PartitionSpec as P

ITERS = 2
TEMPER = 8.0
ROW_AXES = ("z", "y", "xh")
CENT_AXES = ("xl", "core")


def _swap(x, axis, bit):
    size = {"y": 4, "xh": 2}[axis]
    return lax.ppermute(x, axis, [(i, i ^ bit) for i in range(size)])


def _bits():
    y = lax.axis_index("y")
    return ((y & 1, "y", 1), (y >> 1 & 1, "y", 2), (lax.axis_index("xh"), "xh", 1))


def _reduce_rows(numer, mass):
    count, width = numer.shape
    blocks = 8
    per = count // blocks
    mass_rows = (
        jnp.zeros((blocks, 8, width), jnp.float32).at[:, 0, :per].set(mass.reshape(blocks, per))
    )
    payload = jnp.concatenate([numer.reshape(blocks, per, width), mass_rows], axis=1)
    payload = payload.reshape(blocks * (per + 8), width)
    payload = lax.psum_scatter(payload, "z", scatter_dimension=0, tiled=True)
    numer, mass = (payload[:per], payload[per, :per])
    for bit, axis, mask in _bits():
        half = numer.shape[0] // 2
        keep = lax.dynamic_slice_in_dim(numer, bit * half, half, axis=0)
        send = lax.dynamic_slice_in_dim(numer, (1 - bit) * half, half, axis=0)
        keep_mass = lax.dynamic_slice_in_dim(mass, bit * half, half, axis=0)
        send_mass = lax.dynamic_slice_in_dim(mass, (1 - bit) * half, half, axis=0)
        numer = keep + _swap(send, axis, mask)
        mass = keep_mass + _swap(send_mass, axis, mask)
    return (numer, mass)


def _gather_rows(block):
    for bit, axis, mask in reversed(_bits()):
        other = _swap(block, axis, mask)
        block = jnp.where(
            bit == 0, jnp.concatenate([block, other]), jnp.concatenate([other, block])
        )
    return lax.all_gather(block, "z", axis=0, tiled=True)


def _row_offset(count):
    y = lax.axis_index("y")
    per = count // 64
    return (
        lax.axis_index("z") * (count // 8)
        + (y & 1) * (4 * per)
        + (y >> 1 & 1) * (2 * per)
        + lax.axis_index("xh") * per
    )


def _project(embeddings, basis):
    partial = jnp.dot(embeddings, basis, preferred_element_type=jnp.float32)
    steps = ((lax.axis_index("core"), "core"), (lax.axis_index("xl"), "xl"))
    for bit, axis in steps:
        half = partial.shape[0] // 2
        keep = lax.dynamic_slice_in_dim(partial, bit * half, half, axis=0)
        send = lax.dynamic_slice_in_dim(partial, (1 - bit) * half, half, axis=0)
        partial = keep + lax.ppermute(send, axis, [(0, 1), (1, 0)])
    block = partial.astype(jnp.bfloat16)
    for bit, axis in reversed(steps):
        other = lax.ppermute(block, axis, [(0, 1), (1, 0)])
        block = jnp.where(
            bit == 0, jnp.concatenate([block, other]), jnp.concatenate([other, block])
        )
    return block


def _merge(a, b):
    top = jnp.maximum(a[0], b[0])
    return jnp.stack([top, a[1] * jnp.exp(a[0] - top) + b[1] * jnp.exp(b[0] - top)])


def _log_total(scores):
    local_top = jnp.max(scores, axis=1)
    pair = jnp.stack([local_top, jnp.sum(jnp.exp(scores - local_top[:, None]), axis=1)])
    for axis in ("core", "xl"):
        other = lax.ppermute(pair, axis, [(0, 1), (1, 0)])
        low = lax.axis_index(axis) == 0
        pair = _merge(jnp.where(low, pair, other), jnp.where(low, other, pair))
    return pair[0] + jnp.log(pair[1])


def on_device(embeddings, basis, start_centroids):
    row_count = embeddings.shape[0]
    count = start_centroids.shape[0]
    per = count // 64
    projected = _project(embeddings, basis)
    start = _row_offset(count)
    block = lax.dynamic_slice_in_dim(start_centroids, start, per, axis=0)
    cent_bf = start_centroids.astype(jnp.bfloat16)
    log_total = jnp.zeros((row_count,), jnp.float32)
    for step in range(ITERS):
        scores = (
            lax.dot_general(
                projected, cent_bf, (((1,), (1,)), ((), ())), preferred_element_type=jnp.float32
            )
            / TEMPER
        )
        log_total = _log_total(scores)
        weights = jnp.exp(scores - log_total[:, None])
        local_mass = jnp.sum(weights, axis=0)
        local_numer = lax.dot_general(
            weights.astype(jnp.bfloat16),
            projected,
            (((0,), (0,)), ((), ())),
            preferred_element_type=jnp.float32,
        )
        numer, mass = _reduce_rows(local_numer, local_mass)
        block = (numer + block) / (mass[:, None] + 1.0)
        if step + 1 < ITERS:
            cent_bf = _gather_rows(block.astype(jnp.bfloat16))
    centroids = _gather_rows(block)
    return (centroids, log_total)


def solution(mesh):
    fine = Mesh(mesh.devices.reshape(8, 4, 2, 2, 2), ROW_AXES + CENT_AXES)
    return jax.shard_map(
        on_device,
        mesh=fine,
        in_specs=(P(ROW_AXES, CENT_AXES), P(CENT_AXES, None), P(CENT_AXES, None)),
        out_specs=(P(CENT_AXES, None), P(ROW_AXES)),
        check_vma=False,
    )
```

profile of v0, /device:TPU:2, one launch (start us, length us, event | category | flops | bytes accessed | tf_op | source)
XLA Modules:
  0.0 348.0 jit_solution(13008515234022563669)
XLA Ops:
  8.4 4.5 %fusion.34 = f32[2048,512]{1,0:T(8,128)S(1)} fusion(bf16[2048,1024]{1,0:T(8,128)(2,1)} %param.7, bf16[1024,512]{1,0:T(8,128)(2,1)S(1)} %copy-done), kind=kOutput, calls=%fused_computation.95 | convolution fusion | flops 2147483648 | bytes 9437184 | tf_op jit(solution)/shard_map/dot_general | solution.py:66
  15.2 4.3 %collective-permute-done = f32[1024,512]{1,0:T(8,128)} collective-permute-done((f32[1024,512]{1,0:T(8,128)S(1)}, f32[1024,512]{1,0:T(8,128)}, u32[]{:S(2)}, u32[]{:S(2)}) %collective-permute-start) | collective-permute-done | bytes 2097184 | tf_op jit(solution)/shard_map/ppermute | solution.py:72
  19.4 2.7 dynamic-slice_add_fusion
  25.4 23.8 %collective-permute-done.1 = f32[512,512]{1,0:T(8,128)} collective-permute-done((f32[512,512]{1,0:T(8,128)}, f32[512,512]{1,0:T(8,128)}, u32[]{:S(2)}, u32[]{:S(2)}) %collective-permute-start.1) | collective-permute-done | bytes 1048608 | tf_op jit(solution)/shard_map/ppermute | solution.py:72
  53.1 11.9 %collective-permute-done.2 = bf16[512,512]{1,0:T(8,128)(2,1)S(1)} collective-permute-done((bf16[512,512]{1,0:T(8,128)(2,1)}, bf16[512,512]{1,0:T(8,128)(2,1)S(1)}, u32[]{:S(2)}, u32[]{:S(2)}) %collective-permute-start.2) | collective-permute-done | bytes 524320 | tf_op jit(solution)/shard_map/ppermute | solution.py:75
  69.3 4.0 %multiply_reduce_fusion.1 = (f32[2048]{0:T(1024)S(1)}, f32[2048,1024]{0,1:T(8,128)S(1)}) fusion(f32[1024,512]{1,0:T(8,128)} %param.9, bf16[1024,512]{1,0:T(8,128)(2,1)S(1)} %collective-permute-done.3, bf16[1024,512]{1,0:T(8,128)(2,1)S(1)} %maximum_select_fusion.1, pred[]{:T(512)S(6)} %eq.25), kind=kOutput, calls=%fused_computation.9 | convolution fusion | flops 2161637376 | bytes 12591105 | tf_op jit(solution)/shard_map/dot_general | solution.py:108
  85.7 45.1 %reduce-scatter.3.cloned.1.call-done = f32[136,512]{1,0:T(8,128)} async-done(((f32[1088,512]{1,0:T(8,128)}), f32[136,512]{1,0:T(8,128)}) %reduce-scatter.3.cloned.1.call-update) | async-done | bytes 278544 | tf_op jit(solution)/shard_map/reduce_scatter | solution.py:32
  135.3 3.3 collective-permute-start.10
  139.2 2.9 collective-permute-start.7
  147.4 3.1 collective-permute-done.8
  153.6 3.1 collective-permute-done.12
  156.7 2.9 collective-permute-start.13
  163.5 3.0 collective-permute-done.14
  167.5 37.0 %all-gather.3.cloned.1.call-done = bf16[1024,512]{1,0:T(8,128)(2,1)} async-done(((bf16[128,512]{1,0:T(8,128)(2,1)}), bf16[1024,512]{1,0:T(8,128)(2,1)}) %all-gather.3.cloned.1.call-update) | async-done | bytes 1048592 | tf_op jit(solution)/shard_map/all_gather | solution.py:51
  204.6 3.6 %multiply_reduce_fusion = (f32[2048]{0:T(1024)S(1)}, f32[2048,1024]{0,1:T(8,128)S(1)}) fusion(bf16[1024,512]{1,0:T(8,128)(2,1)} %all-gather.3.cloned.1.call-done, bf16[1024,512]{1,0:T(8,128)(2,1)S(1)} %collective-permute-done.3, bf16[1024,512]{1,0:T(8,128)(2,1)S(1)} %maximum_select_fusion.1, pred[]{:T(512)S(6)} %eq.25), kind=kOutput, calls=%fused_computation.8 | convolution fusion | flops 2161113088 | bytes 11542529 | tf_op jit(solution)/shard_map/dot_general | solution.py:108
  211.6 3.2 collective-permute-done.16
  220.5 41.6 %reduce-scatter.5.cloned.1.call-done = f32[136,512]{1,0:T(8,128)} async-done(((f32[1088,512]{1,0:T(8,128)}), f32[136,512]{1,0:T(8,128)}) %reduce-scatter.5.cloned.1.call-update) | async-done | bytes 278544 | tf_op jit(solution)/shard_map/reduce_scatter | solution.py:32
  266.6 2.7 collective-permute-start.21
  278.6 3.4 collective-permute-done.19
  283.7 3.9 %collective-permute-done.23 = f32[16,512]{1,0:T(8,128)S(1)} collective-permute-done((f32[16,512]{1,0:T(8,128)S(1)}, f32[16,512]{1,0:T(8,128)S(1)}, u32[]{:S(2)}, u32[]{:S(2)}) %collective-permute-start.23) | collective-permute-done | bytes 32800 | tf_op jit(solution)/shard_map/ppermute | solution.py:15
  290.2 3.2 collective-permute-done.24
  294.2 4.3 %collective-permute-done.25 = f32[64,512]{1,0:T(8,128)S(1)} collective-permute-done((f32[64,512]{1,0:T(8,128)S(1)}, f32[64,512]{1,0:T(8,128)S(1)}, u32[]{:S(2)}, u32[]{:S(2)}) %collective-permute-start.25) | collective-permute-done | bytes 131104 | tf_op jit(solution)/shard_map/ppermute | solution.py:15
  299.2 39.2 %all-gather.5.cloned.1.call-done = f32[1024,512]{1,0:T(8,128)} async-done(((f32[128,512]{1,0:T(8,128)}), f32[1024,512]{1,0:T(8,128)}) %all-gather.5.cloned.1.call-update) | async-done | bytes 2097168 | tf_op jit(solution)/shard_map/all_gather | solution.py:51
  338.4 3.1 copy.6
  (112 shorter events, 74.2 us)
Async XLA Ops:
  7.2 123.7 %reduce-scatter.3.cloned.1.call-start = ((), (), s32[]{:S(2)}) async-start(), calls=%async_computation.2 | async-start | bytes 2506752 | tf_op jit(solution)/shard_map/reduce_scatter | solution.py:32
  15.1 4.4 %collective-permute-start = (f32[1024,512]{1,0:T(8,128)S(1)}, f32[1024,512]{1,0:T(8,128)}, u32[]{:S(2)}, u32[]{:S(2)}) collective-permute-start(f32[1024,512]{1,0:T(8,128)S(1)} %constant_dynamic-slice_fusion.11), channel_id=1, source_target_pairs={{0,1},{1,0},{2,3},{3,2},{4,5},{5,4},{6,7},{7,6},{8,9},{9,8},{10,11... | collective-permute-start | bytes 6291464 | tf_op jit(solution)/shard_map/ppermute | solution.py:72
  23.2 26.0 %collective-permute-start.1 = (f32[512,512]{1,0:T(8,128)}, f32[512,512]{1,0:T(8,128)}, u32[]{:S(2)}, u32[]{:S(2)}) collective-permute-start(f32[512,512]{1,0:T(8,128)} %constant_dynamic-slice_fusion.10), channel_id=1, source_target_pairs={{0,2},{2,0},{1,3},{3,1},{4,6},{6,4},{5,7},{7,5},{8,10},{10,8},{9,1... | collective-permute-start | bytes 3145736 | tf_op jit(solution)/shard_map/ppermute | solution.py:72
  51.4 13.6 %collective-permute-start.2 = (bf16[512,512]{1,0:T(8,128)(2,1)}, bf16[512,512]{1,0:T(8,128)(2,1)S(1)}, u32[]{:S(2)}, u32[]{:S(2)}) collective-permute-start(bf16[512,512]{1,0:T(8,128)(2,1)} %add_convert_fusion), channel_id=1, source_target_pairs={{0,2},{2,0},{1,3},{3,1},{4,6},{6,4},{5,7},{7,5},{8,10},{10,8},{9,1... | collective-permute-start | bytes 1572872 | tf_op jit(solution)/shard_map/ppermute | solution.py:75
  76.1 4.0 %collective-permute-start.5 = (f32[2,2048]{1,0:T(2,128)S(1)}, f32[2,2048]{1,0:T(2,128)S(1)}, u32[]{:S(2)}, u32[]{:S(2)}) collective-permute-start(f32[2,2048]{1,0:T(2,128)S(1)} %pad_maximum_fusion.1), channel_id=1, source_target_pairs={{0,2},{2,0},{1,3},{3,1},{4,6},{6,4},{5,7},{7,5},{8,10},{10,8},{9,1... | collective-permute-start | bytes 49160 | tf_op jit(solution)/shard_map/ppermute | solution.py:91
  85.6 118.9 %all-gather.3.cloned.1.call-start = ((), (), s32[]{:S(2)}) async-start(), calls=%async_computation.3 | async-start | bytes 1179648 | tf_op jit(solution)/shard_map/all_gather | solution.py:51
  134.1 5.1 %collective-permute-start.6 = (f32[64,512]{1,0:T(8,128)S(1)}, f32[64,512]{1,0:T(8,128)S(1)}, u32[]{:S(2)}, u32[]{:S(2)}) collective-permute-start(f32[64,512]{1,0:T(8,128)S(1)} %constant_dynamic-slice_fusion.9), channel_id=1, source_target_pairs={{0,8},{8,0},{16,24},{24,16},{1,9},{9,1},{17,25},{25,17},{2,10},{10... | collective-permute-start | bytes 393224 | tf_op jit(solution)/shard_map/ppermute | solution.py:15
  135.3 6.8 %collective-permute-start.10 = (f32[32]{0:T(128)S(1)}, f32[32]{0:T(128)S(1)}, u32[]{:S(2)}, u32[]{:S(2)}) collective-permute-start(f32[32]{0:T(128)S(1)} %dynamic_slice.111), channel_id=1, source_target_pairs={{0,16},{8,24},{16,0},{24,8},{1,17},{9,25},{17,1},{25,9},{2,18},{10... | collective-permute-start | bytes 392 | tf_op jit(solution)/shard_map/ppermute | solution.py:15
  139.2 5.9 %collective-permute-start.7 = (f32[32,512]{1,0:T(8,128)S(1)}, f32[32,512]{1,0:T(8,128)S(1)}, u32[]{:S(2)}, u32[]{:S(2)}) collective-permute-start(f32[32,512]{1,0:T(8,128)S(1)} %constant_dynamic-slice_fusion.8), channel_id=1, source_target_pairs={{0,16},{8,24},{16,0},{24,8},{1,17},{9,25},{17,1},{25,9},{2,18},{10... | collective-permute-start | bytes 196616 | tf_op jit(solution)/shard_map/ppermute | solution.py:15
  142.2 5.1 %collective-permute-start.11 = (f32[16]{0:T(128)S(1)}, f32[16]{0:T(128)S(1)}, u32[]{:S(2)}, u32[]{:S(2)}) collective-permute-start(f32[16]{0:T(128)S(1)} %dynamic_slice.113), channel_id=1, source_target_pairs={{0,4},{4,0},{1,5},{5,1},{2,6},{6,2},{3,7},{7,3},{8,12},{12,8},{9,1... | collective-permute-start | bytes 200 | tf_op jit(solution)/shard_map/ppermute | solution.py:15
  145.0 5.5 %collective-permute-start.8 = (f32[16,512]{1,0:T(8,128)S(1)}, f32[16,512]{1,0:T(8,128)S(1)}, u32[]{:S(2)}, u32[]{:S(2)}) collective-permute-start(f32[16,512]{1,0:T(8,128)S(1)} %constant_dynamic-slice_fusion.6), channel_id=1, source_target_pairs={{0,4},{4,0},{1,5},{5,1},{2,6},{6,2},{3,7},{7,3},{8,12},{12,8},{9,1... | collective-permute-start | bytes 98312 | tf_op jit(solution)/shard_map/ppermute | solution.py:15
  151.4 5.3 %collective-permute-start.12 = (bf16[16,512]{1,0:T(8,128)(2,1)S(1)}, bf16[16,512]{1,0:T(8,128)(2,1)S(1)}, u32[]{:S(2)}, u32[]{:S(2)}) collective-permute-start(bf16[16,512]{1,0:T(8,128)(2,1)S(1)} %get-tuple-element.28), channel_id=1, source_target_pairs={{0,4},{4,0},{1,5},{5,1},{2,6},{6,2},{3,7},{7,3},{8,12},{12,8},{9,1... | collective-permute-start | bytes 49160 | tf_op jit(solution)/shard_map/ppermute | solution.py:15
  156.7 5.5 %collective-permute-start.13 = (bf16[32,512]{1,0:T(8,128)(2,1)S(1)}, bf16[32,512]{1,0:T(8,128)(2,1)S(1)}, u32[]{:S(2)}, u32[]{:S(2)}) collective-permute-start(bf16[32,512]{1,0:T(8,128)(2,1)S(1)} %maximum_select_fusion.7), channel_id=1, source_target_pairs={{0,16},{8,24},{16,0},{24,8},{1,17},{9,25},{17,1},{25,9},{2,18},{10... | collective-permute-start | bytes 98312 | tf_op jit(solution)/shard_map/ppermute | solution.py:15
  162.2 4.4 %collective-permute-start.14 = (bf16[64,512]{1,0:T(8,128)(2,1)S(1)}, bf16[64,512]{1,0:T(8,128)(2,1)S(1)}, u32[]{:S(2)}, u32[]{:S(2)}) collective-permute-start(bf16[64,512]{1,0:T(8,128)(2,1)S(1)} %maximum_select_fusion.5), channel_id=1, source_target_pairs={{0,8},{8,0},{16,24},{24,16},{1,9},{9,1},{17,25},{25,17},{2,10},{10... | collective-permute-start | bytes 196616 | tf_op jit(solution)/shard_map/ppermute | solution.py:15
  167.3 94.8 %reduce-scatter.5.cloned.1.call-start = ((), (), s32[]{:S(2)}) async-start(), calls=%async_computation.4 | async-start | bytes 2506752 | tf_op jit(solution)/shard_map/reduce_scatter | solution.py:32
  220.4 118.0 %all-gather.5.cloned.1.call-start = ((), (), s32[]{:S(2)}) async-start(), calls=%async_computation.5 | async-start | bytes 2359296 | tf_op jit(solution)/shard_map/all_gather | solution.py:51
  265.5 5.1 %collective-permute-start.17 = (f32[64,512]{1,0:T(8,128)S(1)}, f32[64,512]{1,0:T(8,128)S(1)}, u32[]{:S(2)}, u32[]{:S(2)}) collective-permute-start(f32[64,512]{1,0:T(8,128)S(1)} %constant_dynamic-slice_fusion.3), channel_id=1, source_target_pairs={{0,8},{8,0},{16,24},{24,16},{1,9},{9,1},{17,25},{25,17},{2,10},{10... | collective-permute-start | bytes 393224 | tf_op jit(solution)/shard_map/ppermute | solution.py:15
  266.6 6.8 %collective-permute-start.21 = (f32[32]{0:T(128)S(1)}, f32[32]{0:T(128)S(1)}, u32[]{:S(2)}, u32[]{:S(2)}) collective-permute-start(f32[32]{0:T(128)S(1)} %dynamic_slice.125), channel_id=1, source_target_pairs={{0,16},{8,24},{16,0},{24,8},{1,17},{9,25},{17,1},{25,9},{2,18},{10... | collective-permute-start | bytes 392 | tf_op jit(solution)/shard_map/ppermute | solution.py:15
  270.6 5.9 %collective-permute-start.18 = (f32[32,512]{1,0:T(8,128)S(1)}, f32[32,512]{1,0:T(8,128)S(1)}, u32[]{:S(2)}, u32[]{:S(2)}) collective-permute-start(f32[32,512]{1,0:T(8,128)S(1)} %constant_dynamic-slice_fusion.2), channel_id=1, source_target_pairs={{0,16},{8,24},{16,0},{24,8},{1,17},{9,25},{17,1},{25,9},{2,18},{10... | collective-permute-start | bytes 196616 | tf_op jit(solution)/shard_map/ppermute | solution.py:15
  273.5 5.1 %collective-permute-start.22 = (f32[16]{0:T(128)S(1)}, f32[16]{0:T(128)S(1)}, u32[]{:S(2)}, u32[]{:S(2)}) collective-permute-start(f32[16]{0:T(128)S(1)} %dynamic_slice.127), channel_id=1, source_target_pairs={{0,4},{4,0},{1,5},{5,1},{2,6},{6,2},{3,7},{7,3},{8,12},{12,8},{9,1... | collective-permute-start | bytes 200 | tf_op jit(solution)/shard_map/ppermute | solution.py:15
  276.5 5.5 %collective-permute-start.19 = (f32[16,512]{1,0:T(8,128)S(1)}, f32[16,512]{1,0:T(8,128)S(1)}, u32[]{:S(2)}, u32[]{:S(2)}) collective-permute-start(f32[16,512]{1,0:T(8,128)S(1)} %constant_dynamic-slice_fusion.1), channel_id=1, source_target_pairs={{0,4},{4,0},{1,5},{5,1},{2,6},{6,2},{3,7},{7,3},{8,12},{12,8},{9,1... | collective-permute-start | bytes 98312 | tf_op jit(solution)/shard_map/ppermute | solution.py:15
  282.1 5.4 %collective-permute-start.23 = (f32[16,512]{1,0:T(8,128)S(1)}, f32[16,512]{1,0:T(8,128)S(1)}, u32[]{:S(2)}, u32[]{:S(2)}) collective-permute-start(f32[16,512]{1,0:T(8,128)S(1)} %add_divide_fusion), channel_id=1, source_target_pairs={{0,4},{4,0},{1,5},{5,1},{2,6},{6,2},{3,7},{7,3},{8,12},{12,8},{9,1... | collective-permute-start | bytes 98312 | tf_op jit(solution)/shard_map/ppermute | solution.py:15
  287.6 5.9 %collective-permute-start.24 = (f32[32,512]{1,0:T(8,128)S(1)}, f32[32,512]{1,0:T(8,128)S(1)}, u32[]{:S(2)}, u32[]{:S(2)}) collective-permute-start(f32[32,512]{1,0:T(8,128)S(1)} %maximum_select_fusion.6), channel_id=1, source_target_pairs={{0,16},{8,24},{16,0},{24,8},{1,17},{9,25},{17,1},{25,9},{2,18},{10... | collective-permute-start | bytes 196616 | tf_op jit(solution)/shard_map/ppermute | solution.py:15
  293.4 5.1 %collective-permute-start.25 = (f32[64,512]{1,0:T(8,128)S(1)}, f32[64,512]{1,0:T(8,128)S(1)}, u32[]{:S(2)}, u32[]{:S(2)}) collective-permute-start(f32[64,512]{1,0:T(8,128)S(1)} %maximum_select_fusion.4), channel_id=1, source_target_pairs={{0,8},{8,0},{16,24},{24,16},{1,9},{9,1},{17,25},{25,17},{2,10},{10... | collective-permute-start | bytes 393224 | tf_op jit(solution)/shard_map/ppermute | solution.py:15
  (9 other events, 20.9 us)
Sparse Core Ops, SparseCore 0:
  85.7 45.0 reduce-scatter.2
  167.4 37.1 all-gather.2
  220.5 41.5 reduce-scatter.4
  299.4 39.0 all-gather.4
where the time goes:
time: 349 us; the launch traced here: 348 us
  waiting for transfers between devices  245 us (70%)
  starting transfers between devices  42.1 us (12%)
  other arithmetic  18.4 us (5%)
  matrix products  16.9 us (5%)
  between operations  14.1 us (4%)
  local copies, waits for them, and re-layouts  11.3 us (3%)
    reduce_scatter x2, waiting for transfers between devices, _reduce_rows(): payload = lax.psum_scatter(payload, 'z', scatter_dimension=0, tiled=True)  86.8 us
    all_gather x2, waiting for transfers between devices, _gather_rows(): return lax.all_gather(block, 'z', axis=0, tiled=True)  76.2 us
    ppermute x18, starting transfers between devices, _swap(): return lax.ppermute(x, axis, [(i, i ^ bit) for i in range(size)])  34.9 us
    ppermute x18, waiting for transfers between devices, _swap(): return lax.ppermute(x, axis, [(i, i ^ bit) for i in range(size)])  31.9 us
    ppermute x2, waiting for transfers between devices, _project(): partial = keep + lax.ppermute(send, axis, [(0, 1), (1, 0)])  28 us
    ppermute x2, waiting for transfers between devices, _project(): other = lax.ppermute(block, axis, [(0, 1), (1, 0)])  14.5 us
    ppermute x4, waiting for transfers between devices, _log_total(): other = lax.ppermute(pair, axis, [(0, 1), (1, 0)])  7.67 us
    dot_general x2, matrix products, on_device(): lax.dot_general(projected, cent_bf, (((1,), (1,)), ((), ())), preferred_e...  7.58 us
  transfers between devices with their start and end apart: 30, of which 27 were waited for; matrix products, arithmetic and copies ran while one was open for 1% of the time, Pallas kernels for 0%

commit v1 on v0

--- a/solution.py
+++ b/solution.py
@@ -48,7 +48,9 @@
         block = jnp.where(
             bit == 0, jnp.concatenate([block, other]), jnp.concatenate([other, block])
         )
-    return lax.all_gather(block, "z", axis=0, tiled=True)
+    return jnp.concatenate(
+        lax.all_to_all(jnp.stack([block] * lax.axis_size("z")), "z", 0, 0), axis=0
+    )
 
 
 def _row_offset(count):

time: 349 us -> 334 us (0.957)
  waiting for transfers between devices: 245 us -> 164 us
  blocking collectives: 0 us -> 69.1 us
    all_gather x2 -> x0, waiting for transfers between devices: 76.2 us -> none  [_gather_rows(): return lax.all_gather(block, 'z', axis=0, tiled=True)]
    all_to_all x0 -> x2, blocking collectives: none -> 69.1 us  [_gather_rows(): lax.all_to_all(jnp.stack([block] * lax.axis_size('z')), 'z', 0, 0)]
  transfers between devices with their start and end apart: 30 -> 28, of which waited for: 27 -> 24; matrix products, arithmetic and copies ran while one was open for 1% -> 1% of each run, Pallas kernels for 0% -> 0%
where the time goes in v1:
time: 334 us
  waiting for transfers between devices  164 us (49%)
  blocking collectives  69.1 us (21%)
  starting transfers between devices  43.4 us (13%)
  other arithmetic  17.1 us (5%)
  matrix products  15.7 us (5%)
  between operations  14.4 us (4%)
  local copies, waits for them, and re-layouts  9.86 us (3%)
    reduce_scatter x2, waiting for transfers between devices, _reduce_rows(): payload = lax.psum_scatter(payload, 'z', scatter_dimension=0, tiled=True)  83.5 us
    all_to_all x2, blocking collectives, _gather_rows(): lax.all_to_all(jnp.stack([block] * lax.axis_size('z')), 'z', 0, 0)  69.1 us
    ppermute x18, starting transfers between devices, _swap(): return lax.ppermute(x, axis, [(i, i ^ bit) for i in range(size)])  36.7 us
    ppermute x18, waiting for transfers between devices, _swap(): return lax.ppermute(x, axis, [(i, i ^ bit) for i in range(size)])  29.9 us
    ppermute x2, waiting for transfers between devices, _project(): partial = keep + lax.ppermute(send, axis, [(0, 1), (1, 0)])  28 us
    ppermute x2, waiting for transfers between devices, _project(): other = lax.ppermute(block, axis, [(0, 1), (1, 0)])  14.5 us
    ppermute x4, waiting for transfers between devices, _log_total(): other = lax.ppermute(pair, axis, [(0, 1), (1, 0)])  7.96 us
  transfers between devices with their start and end apart: 28, of which 24 were waited for; matrix products, arithmetic and copies ran while one was open for 1% of the time, Pallas kernels for 0%

profile of v1, /device:TPU:2, one launch (start us, length us, event | category | flops | bytes accessed | tf_op | source)
XLA Modules:
  0.0 333.5 jit_solution(8118744879258195521)
XLA Ops:
  8.4 4.5 %fusion.34 = f32[2048,512]{1,0:T(8,128)S(1)} fusion(bf16[2048,1024]{1,0:T(8,128)(2,1)} %param.7, bf16[1024,512]{1,0:T(8,128)(2,1)S(1)} %copy-done), kind=kOutput, calls=%fused_computation.95 | convolution fusion | flops 2147483648 | bytes 9437184 | tf_op jit(solution)/shard_map/dot_general | solution.py:68
  15.2 4.3 %collective-permute-done = f32[1024,512]{1,0:T(8,128)} collective-permute-done((f32[1024,512]{1,0:T(8,128)S(1)}, f32[1024,512]{1,0:T(8,128)}, u32[]{:S(2)}, u32[]{:S(2)}) %collective-permute-start) | collective-permute-done | bytes 2097184 | tf_op jit(solution)/shard_map/ppermute | solution.py:74
  19.4 2.7 dynamic-slice_add_fusion
  25.4 23.8 %collective-permute-done.1 = f32[512,512]{1,0:T(8,128)} collective-permute-done((f32[512,512]{1,0:T(8,128)}, f32[512,512]{1,0:T(8,128)}, u32[]{:S(2)}, u32[]{:S(2)}) %collective-permute-start.1) | collective-permute-done | bytes 1048608 | tf_op jit(solution)/shard_map/ppermute | solution.py:74
  53.1 11.9 %collective-permute-done.2 = bf16[512,512]{1,0:T(8,128)(2,1)S(1)} collective-permute-done((bf16[512,512]{1,0:T(8,128)(2,1)}, bf16[512,512]{1,0:T(8,128)(2,1)S(1)}, u32[]{:S(2)}, u32[]{:S(2)}) %collective-permute-start.2) | collective-permute-done | bytes 524320 | tf_op jit(solution)/shard_map/ppermute | solution.py:77
  69.3 4.0 %multiply_reduce_fusion.1 = (f32[2048]{0:T(1024)S(1)}, f32[2048,1024]{0,1:T(8,128)S(1)}) fusion(f32[1024,512]{1,0:T(8,128)} %param.9, bf16[1024,512]{1,0:T(8,128)(2,1)S(1)} %collective-permute-done.3, bf16[1024,512]{1,0:T(8,128)(2,1)S(1)} %maximum_select_fusion.1, pred[]{:T(512)S(6)} %eq.25), kind=kOutput, calls=%fused_computation.9 | convolution fusion | flops 2161637376 | bytes 12591105 | tf_op jit(solution)/shard_map/dot_general | solution.py:110
  85.7 45.1 %reduce-scatter.3.cloned.1.call-done = f32[136,512]{1,0:T(8,128)} async-done(((f32[1088,512]{1,0:T(8,128)}), f32[136,512]{1,0:T(8,128)}) %reduce-scatter.3.cloned.1.call-update) | async-done | bytes 278544 | tf_op jit(solution)/shard_map/reduce_scatter | solution.py:32
  135.3 3.3 collective-permute-start.10
  139.1 2.9 collective-permute-start.7
  147.4 3.1 collective-permute-done.8
  153.6 3.1 collective-permute-done.12
  156.7 2.9 collective-permute-start.13
  163.5 3.0 collective-permute-done.14
  166.6 24.1 %all_to_all.10 = bf16[8,128,512]{2,1,0:T(8,128)(2,1)S(1)} all-to-all(bf16[8,128,512]{2,1,0:T(8,128)(2,1)S(1)} %stack.24), channel_id=1, replica_groups=mesh['z'=8,'y'=4,'xh'=2,'xl'=2,'core'=2] {'z'}, dimensions={0} | all-to-all | bytes 2097152 | tf_op jit(solution)/shard_map/all_to_all | solution.py:52
  196.3 3.5 %collective-permute-done.16 = f32[2,2048]{1,0:T(2,128)S(1)} collective-permute-done((f32[2,2048]{1,0:T(2,128)S(1)}, f32[2,2048]{1,0:T(2,128)S(1)}, u32[]{:S(2)}, u32[]{:S(2)}) %collective-permute-start.16) | collective-permute-done | bytes 16416 | tf_op jit(solution)/shard_map/ppermute | solution.py:93
  205.3 38.4 %reduce-scatter.5.cloned.1.call-done = f32[136,512]{1,0:T(8,128)} async-done(((f32[1088,512]{1,0:T(8,128)}), f32[136,512]{1,0:T(8,128)}) %reduce-scatter.5.cloned.1.call-update) | async-done | bytes 278544 | tf_op jit(solution)/shard_map/reduce_scatter | solution.py:32
  248.2 3.0 collective-permute-start.21
  252.2 2.7 collective-permute-start.18
  260.2 3.4 %collective-permute-done.19 = f32[16,512]{1,0:T(8,128)S(1)} collective-permute-done((f32[16,512]{1,0:T(8,128)S(1)}, f32[16,512]{1,0:T(8,128)S(1)}, u32[]{:S(2)}, u32[]{:S(2)}) %collective-permute-start.19) | collective-permute-done | bytes 32800 | tf_op jit(solution)/shard_map/ppermute | solution.py:15
  265.6 3.5 %collective-permute-done.23 = f32[16,512]{1,0:T(8,128)S(1)} collective-permute-done((f32[16,512]{1,0:T(8,128)S(1)}, f32[16,512]{1,0:T(8,128)S(1)}, u32[]{:S(2)}, u32[]{:S(2)}) %collective-permute-start.23) | collective-permute-done | bytes 32800 | tf_op jit(solution)/shard_map/ppermute | solution.py:15
  269.1 2.7 collective-permute-start.24
  271.8 3.2 collective-permute-done.24
  276.2 3.9 %collective-permute-done.25 = f32[64,512]{1,0:T(8,128)S(1)} collective-permute-done((f32[64,512]{1,0:T(8,128)S(1)}, f32[64,512]{1,0:T(8,128)S(1)}, u32[]{:S(2)}, u32[]{:S(2)}) %collective-permute-start.25) | collective-permute-done | bytes 131104 | tf_op jit(solution)/shard_map/ppermute | solution.py:15
  280.3 45.0 %all_to_all.11 = f32[8,128,512]{2,1,0:T(8,128)S(1)} all-to-all(f32[8,128,512]{2,1,0:T(8,128)S(1)} %stack.29), channel_id=1, replica_groups=mesh['z'=8,'y'=4,'xh'=2,'xl'=2,'core'=2] {'z'}, dimensions={0} | all-to-all | bytes 4194304 | tf_op jit(solution)/shard_map/all_to_all | solution.py:52
  (110 shorter events, 71.3 us)
Async XLA Ops:
  7.2 123.6 %reduce-scatter.3.cloned.1.call-start = ((), (), s32[]{:S(2)}) async-start(), calls=%async_computation.4 | async-start | bytes 2506752 | tf_op jit(solution)/shard_map/reduce_scatter | solution.py:32
  15.0 4.4 %collective-permute-start = (f32[1024,512]{1,0:T(8,128)S(1)}, f32[1024,512]{1,0:T(8,128)}, u32[]{:S(2)}, u32[]{:S(2)}) collective-permute-start(f32[1024,512]{1,0:T(8,128)S(1)} %constant_dynamic-slice_fusion.11), channel_id=1, source_target_pairs={{0,1},{1,0},{2,3},{3,2},{4,5},{5,4},{6,7},{7,6},{8,9},{9,8},{10,11... | collective-permute-start | bytes 6291464 | tf_op jit(solution)/shard_map/ppermute | solution.py:74
  23.2 26.0 %collective-permute-start.1 = (f32[512,512]{1,0:T(8,128)}, f32[512,512]{1,0:T(8,128)}, u32[]{:S(2)}, u32[]{:S(2)}) collective-permute-start(f32[512,512]{1,0:T(8,128)} %constant_dynamic-slice_fusion.10), channel_id=1, source_target_pairs={{0,2},{2,0},{1,3},{3,1},{4,6},{6,4},{5,7},{7,5},{8,10},{10,8},{9,1... | collective-permute-start | bytes 3145736 | tf_op jit(solution)/shard_map/ppermute | solution.py:74
  51.4 13.6 %collective-permute-start.2 = (bf16[512,512]{1,0:T(8,128)(2,1)}, bf16[512,512]{1,0:T(8,128)(2,1)S(1)}, u32[]{:S(2)}, u32[]{:S(2)}) collective-permute-start(bf16[512,512]{1,0:T(8,128)(2,1)} %add_convert_fusion), channel_id=1, source_target_pairs={{0,2},{2,0},{1,3},{3,1},{4,6},{6,4},{5,7},{7,5},{8,10},{10,8},{9,1... | collective-permute-start | bytes 1572872 | tf_op jit(solution)/shard_map/ppermute | solution.py:77
  76.1 4.0 %collective-permute-start.5 = (f32[2,2048]{1,0:T(2,128)S(1)}, f32[2,2048]{1,0:T(2,128)S(1)}, u32[]{:S(2)}, u32[]{:S(2)}) collective-permute-start(f32[2,2048]{1,0:T(2,128)S(1)} %pad_maximum_fusion.1), channel_id=1, source_target_pairs={{0,2},{2,0},{1,3},{3,1},{4,6},{6,4},{5,7},{7,5},{8,10},{10,8},{9,1... | collective-permute-start | bytes 49160 | tf_op jit(solution)/shard_map/ppermute | solution.py:93
  85.6 158.1 %reduce-scatter.5.cloned.1.call-start = ((), (), s32[]{:S(2)}) async-start(), calls=%async_computation.5 | async-start | bytes 2506752 | tf_op jit(solution)/shard_map/reduce_scatter | solution.py:32
  131.6 3.6 %collective-permute-start.9 = (f32[64]{0:T(128)S(1)}, f32[64]{0:T(128)S(1)}, u32[]{:S(2)}, u32[]{:S(2)}) collective-permute-start(f32[64]{0:T(128)S(1)} %fusion.23), channel_id=1, source_target_pairs={{0,8},{8,0},{16,24},{24,16},{1,9},{9,1},{17,25},{25,17},{2,10},{10... | collective-permute-start | bytes 776 | tf_op jit(solution)/shard_map/ppermute | solution.py:15
  134.0 5.1 %collective-permute-start.6 = (f32[64,512]{1,0:T(8,128)S(1)}, f32[64,512]{1,0:T(8,128)S(1)}, u32[]{:S(2)}, u32[]{:S(2)}) collective-permute-start(f32[64,512]{1,0:T(8,128)S(1)} %constant_dynamic-slice_fusion.9), channel_id=1, source_target_pairs={{0,8},{8,0},{16,24},{24,16},{1,9},{9,1},{17,25},{25,17},{2,10},{10... | collective-permute-start | bytes 393224 | tf_op jit(solution)/shard_map/ppermute | solution.py:15
  135.3 6.8 %collective-permute-start.10 = (f32[32]{0:T(128)S(1)}, f32[32]{0:T(128)S(1)}, u32[]{:S(2)}, u32[]{:S(2)}) collective-permute-start(f32[32]{0:T(128)S(1)} %dynamic_slice.111), channel_id=1, source_target_pairs={{0,16},{8,24},{16,0},{24,8},{1,17},{9,25},{17,1},{25,9},{2,18},{10... | collective-permute-start | bytes 392 | tf_op jit(solution)/shard_map/ppermute | solution.py:15
  139.1 5.9 %collective-permute-start.7 = (f32[32,512]{1,0:T(8,128)S(1)}, f32[32,512]{1,0:T(8,128)S(1)}, u32[]{:S(2)}, u32[]{:S(2)}) collective-permute-start(f32[32,512]{1,0:T(8,128)S(1)} %constant_dynamic-slice_fusion.8), channel_id=1, source_target_pairs={{0,16},{8,24},{16,0},{24,8},{1,17},{9,25},{17,1},{25,9},{2,18},{10... | collective-permute-start | bytes 196616 | tf_op jit(solution)/shard_map/ppermute | solution.py:15
  142.2 5.1 %collective-permute-start.11 = (f32[16]{0:T(128)S(1)}, f32[16]{0:T(128)S(1)}, u32[]{:S(2)}, u32[]{:S(2)}) collective-permute-start(f32[16]{0:T(128)S(1)} %dynamic_slice.113), channel_id=1, source_target_pairs={{0,4},{4,0},{1,5},{5,1},{2,6},{6,2},{3,7},{7,3},{8,12},{12,8},{9,1... | collective-permute-start | bytes 200 | tf_op jit(solution)/shard_map/ppermute | solution.py:15
  145.0 5.5 %collective-permute-start.8 = (f32[16,512]{1,0:T(8,128)S(1)}, f32[16,512]{1,0:T(8,128)S(1)}, u32[]{:S(2)}, u32[]{:S(2)}) collective-permute-start(f32[16,512]{1,0:T(8,128)S(1)} %constant_dynamic-slice_fusion.6), channel_id=1, source_target_pairs={{0,4},{4,0},{1,5},{5,1},{2,6},{6,2},{3,7},{7,3},{8,12},{12,8},{9,1... | collective-permute-start | bytes 98312 | tf_op jit(solution)/shard_map/ppermute | solution.py:15
  151.4 5.3 %collective-permute-start.12 = (bf16[16,512]{1,0:T(8,128)(2,1)S(1)}, bf16[16,512]{1,0:T(8,128)(2,1)S(1)}, u32[]{:S(2)}, u32[]{:S(2)}) collective-permute-start(bf16[16,512]{1,0:T(8,128)(2,1)S(1)} %get-tuple-element.28), channel_id=1, source_target_pairs={{0,4},{4,0},{1,5},{5,1},{2,6},{6,2},{3,7},{7,3},{8,12},{12,8},{9,1... | collective-permute-start | bytes 49160 | tf_op jit(solution)/shard_map/ppermute | solution.py:15
  156.7 5.5 %collective-permute-start.13 = (bf16[32,512]{1,0:T(8,128)(2,1)S(1)}, bf16[32,512]{1,0:T(8,128)(2,1)S(1)}, u32[]{:S(2)}, u32[]{:S(2)}) collective-permute-start(bf16[32,512]{1,0:T(8,128)(2,1)S(1)} %maximum_select_fusion.7), channel_id=1, source_target_pairs={{0,16},{8,24},{16,0},{24,8},{1,17},{9,25},{17,1},{25,9},{2,18},{10... | collective-permute-start | bytes 98312 | tf_op jit(solution)/shard_map/ppermute | solution.py:15
  162.2 4.4 %collective-permute-start.14 = (bf16[64,512]{1,0:T(8,128)(2,1)S(1)}, bf16[64,512]{1,0:T(8,128)(2,1)S(1)}, u32[]{:S(2)}, u32[]{:S(2)}) collective-permute-start(bf16[64,512]{1,0:T(8,128)(2,1)S(1)} %maximum_select_fusion.5), channel_id=1, source_target_pairs={{0,8},{8,0},{16,24},{24,16},{1,9},{9,1},{17,25},{25,17},{2,10},{10... | collective-permute-start | bytes 196616 | tf_op jit(solution)/shard_map/ppermute | solution.py:15
  195.9 3.8 %collective-permute-start.16 = (f32[2,2048]{1,0:T(2,128)S(1)}, f32[2,2048]{1,0:T(2,128)S(1)}, u32[]{:S(2)}, u32[]{:S(2)}) collective-permute-start(f32[2,2048]{1,0:T(2,128)S(1)} %pad_maximum_fusion.3), channel_id=1, source_target_pairs={{0,2},{2,0},{1,3},{3,1},{4,6},{6,4},{5,7},{7,5},{8,10},{10,8},{9,1... | collective-permute-start | bytes 49160 | tf_op jit(solution)/shard_map/ppermute | solution.py:93
  246.9 5.2 %collective-permute-start.17 = (f32[64,512]{1,0:T(8,128)S(1)}, f32[64,512]{1,0:T(8,128)S(1)}, u32[]{:S(2)}, u32[]{:S(2)}) collective-permute-start(f32[64,512]{1,0:T(8,128)S(1)} %constant_dynamic-slice_fusion.3), channel_id=1, source_target_pairs={{0,8},{8,0},{16,24},{24,16},{1,9},{9,1},{17,25},{25,17},{2,10},{10... | collective-permute-start | bytes 393224 | tf_op jit(solution)/shard_map/ppermute | solution.py:15
  248.2 6.7 %collective-permute-start.21 = (f32[32]{0:T(128)S(1)}, f32[32]{0:T(128)S(1)}, u32[]{:S(2)}, u32[]{:S(2)}) collective-permute-start(f32[32]{0:T(128)S(1)} %dynamic_slice.125), channel_id=1, source_target_pairs={{0,16},{8,24},{16,0},{24,8},{1,17},{9,25},{17,1},{25,9},{2,18},{10... | collective-permute-start | bytes 392 | tf_op jit(solution)/shard_map/ppermute | solution.py:15
  252.2 5.9 %collective-permute-start.18 = (f32[32,512]{1,0:T(8,128)S(1)}, f32[32,512]{1,0:T(8,128)S(1)}, u32[]{:S(2)}, u32[]{:S(2)}) collective-permute-start(f32[32,512]{1,0:T(8,128)S(1)} %constant_dynamic-slice_fusion.2), channel_id=1, source_target_pairs={{0,16},{8,24},{16,0},{24,8},{1,17},{9,25},{17,1},{25,9},{2,18},{10... | collective-permute-start | bytes 196616 | tf_op jit(solution)/shard_map/ppermute | solution.py:15
  255.0 5.1 %collective-permute-start.22 = (f32[16]{0:T(128)S(1)}, f32[16]{0:T(128)S(1)}, u32[]{:S(2)}, u32[]{:S(2)}) collective-permute-start(f32[16]{0:T(128)S(1)} %dynamic_slice.127), channel_id=1, source_target_pairs={{0,4},{4,0},{1,5},{5,1},{2,6},{6,2},{3,7},{7,3},{8,12},{12,8},{9,1... | collective-permute-start | bytes 200 | tf_op jit(solution)/shard_map/ppermute | solution.py:15
  258.1 5.5 %collective-permute-start.19 = (f32[16,512]{1,0:T(8,128)S(1)}, f32[16,512]{1,0:T(8,128)S(1)}, u32[]{:S(2)}, u32[]{:S(2)}) collective-permute-start(f32[16,512]{1,0:T(8,128)S(1)} %constant_dynamic-slice_fusion.1), channel_id=1, source_target_pairs={{0,4},{4,0},{1,5},{5,1},{2,6},{6,2},{3,7},{7,3},{8,12},{12,8},{9,1... | collective-permute-start | bytes 98312 | tf_op jit(solution)/shard_map/ppermute | solution.py:15
  263.7 5.4 %collective-permute-start.23 = (f32[16,512]{1,0:T(8,128)S(1)}, f32[16,512]{1,0:T(8,128)S(1)}, u32[]{:S(2)}, u32[]{:S(2)}) collective-permute-start(f32[16,512]{1,0:T(8,128)S(1)} %add_divide_fusion), channel_id=1, source_target_pairs={{0,4},{4,0},{1,5},{5,1},{2,6},{6,2},{3,7},{7,3},{8,12},{12,8},{9,1... | collective-permute-start | bytes 98312 | tf_op jit(solution)/shard_map/ppermute | solution.py:15
  269.1 5.9 %collective-permute-start.24 = (f32[32,512]{1,0:T(8,128)S(1)}, f32[32,512]{1,0:T(8,128)S(1)}, u32[]{:S(2)}, u32[]{:S(2)}) collective-permute-start(f32[32,512]{1,0:T(8,128)S(1)} %maximum_select_fusion.6), channel_id=1, source_target_pairs={{0,16},{8,24},{16,0},{24,8},{1,17},{9,25},{17,1},{25,9},{2,18},{10... | collective-permute-start | bytes 196616 | tf_op jit(solution)/shard_map/ppermute | solution.py:15
  275.0 5.1 %collective-permute-start.25 = (f32[64,512]{1,0:T(8,128)S(1)}, f32[64,512]{1,0:T(8,128)S(1)}, u32[]{:S(2)}, u32[]{:S(2)}) collective-permute-start(f32[64,512]{1,0:T(8,128)S(1)} %maximum_select_fusion.4), channel_id=1, source_target_pairs={{0,8},{8,0},{16,24},{24,16},{1,9},{9,1},{17,25},{25,17},{2,10},{10... | collective-permute-start | bytes 393224 | tf_op jit(solution)/shard_map/ppermute | solution.py:15
  (7 other events, 13.5 us)
Sparse Core Ops, SparseCore 0:
  85.7 45.0 reduce-scatter.2
  205.4 38.2 reduce-scatter.4
